TPU v7x, 128 devices: a whole 4x4x4 slice. The times are simulated.
128 devices in a mesh: dp: 32 (over x, y, core), tensor: 4 (over z).
Axes of the slice: x: 4, y: 4, z: 4, core: 2. Of those that a mesh axis runs over, the one named last changes fastest.
Arguments:
- query: bfloat16 [32768, 5120], P('dp', 'tensor'), may hold values from -6 to 6
- keys: bfloat16 [32768, 1024], P('dp', 'tensor'), may hold values from -6 to 6
- values: bfloat16 [32768, 1024], P('dp', 'tensor'), may hold values from -6 to 6
- out_weight: bfloat16 [5120, 2560], P('tensor', 'dp'), may hold values from -0.078125 to 0.078125
- loss_grad: bfloat16 [32768, 2560], P('dp', 'tensor'), may hold values from -6 to 6
- lengths: int32 [32, 16], P('dp'), may hold values from 1 to 512, 1024 in all within a row
- languages: int32 [32, 16], P('dp'), may hold values from 0 to 28
- labels: int32 [32768], P('dp'), may hold values from -100 to 152063, as said below
Outputs:
- attention_result: bfloat16 [32768, 5120], P('dp', 'tensor')
- query_gradient: bfloat16 [32768, 5120], P('dp', 'tensor')
- key_gradient: bfloat16 [32768, 1024], P('dp', 'tensor')
- value_gradient: bfloat16 [32768, 1024], P('dp', 'tensor')
- projection_gradient: bfloat16 [5120, 2560], P('tensor')
Inputs may be any that keep to these rules, and one draw needn't show every extreme that they name: `labels`: each label is -100, meaning no loss on that token, or a token id below 152064.
All inputs are finite; a program needn't handle non-finite values.
Results may differ from a plain program's by a relative error of at most 0.02.
Values may be sent and summed in bfloat16 or wider, within the bound.
No kernel may reach another device: no remote copies, remote signals or barrier semaphores. Data moves between devices by JAX's collectives and lax.ppermute only.
A program may use at most 192 MiB of HBM per device.

v0:
```python
import functools
import math

import jax
import jax.numpy as jnp
from jax import lax
from jax.experimental import pallas as pl
from jax.experimental.pallas import tpu as pltpu
from jax.sharding import PartitionSpec as P


QUERY_HEADS = 40
KEY_VALUE_HEADS = 8
HEAD_SIZE = 128
LANGS = 29
DOCS = 16
COUNT_BASE = 32


def token_docs(length_row, row_count):
    doc_ends = jnp.cumsum(length_row)
    places = jnp.arange(row_count, dtype=jnp.int32)
    return jnp.sum((places[:, None] >= doc_ends[None, :]).astype(jnp.int32), axis=1)


GROUP = QUERY_HEADS // KEY_VALUE_HEADS
ROW_BLOCK = 256
MASKED = -1e30
NT_DIMS = (((1,), (1,)), ((), ()))


def block_mask(row_doc_ref, col_doc_ref, first_row, key_end):
    row_doc = row_doc_ref[first_row : first_row + ROW_BLOCK, :]
    col_doc = col_doc_ref[:, :key_end]
    shape = (ROW_BLOCK, key_end)
    rows = lax.broadcasted_iota(jnp.int32, shape, 0) + first_row
    cols = lax.broadcasted_iota(jnp.int32, shape, 1)
    return (row_doc == col_doc) & (cols <= rows)


def forward_kernel(factor, q_ref, k_ref, v_ref, row_doc_ref, col_doc_ref, o_ref, lse_ref):
    row_count = q_ref.shape[0]
    for block in range(row_count // ROW_BLOCK):
        first_row = block * ROW_BLOCK
        key_end = first_row + ROW_BLOCK
        allowed = block_mask(row_doc_ref, col_doc_ref, first_row, key_end)
        rows = pl.ds(first_row, ROW_BLOCK)

        def head_body(head, carry):
            cols = pl.ds(pl.multiple_of(head * HEAD_SIZE, HEAD_SIZE), HEAD_SIZE)
            query = q_ref[rows, cols]
            scores = lax.dot_general(
                query, k_ref[:key_end, :], NT_DIMS, preferred_element_type=jnp.float32
            ) * factor
            scores = jnp.where(allowed, scores, MASKED)
            top = jnp.max(scores, axis=1, keepdims=True)
            log_total = top + jnp.log(jnp.sum(jnp.exp(scores - top), axis=1, keepdims=True))
            weights = jnp.exp(scores - log_total).astype(jnp.bfloat16)
            result = jnp.dot(weights, v_ref[:key_end, :], preferred_element_type=jnp.float32)
            o_ref[rows, cols] = result.astype(o_ref.dtype)
            lse_ref[0, head, rows, :] = jnp.broadcast_to(log_total, (ROW_BLOCK, HEAD_SIZE))
            return carry

        lax.fori_loop(0, GROUP, head_body, 0)


def backward_kernel(
    factor, q_ref, k_ref, v_ref, row_doc_ref, col_doc_ref, o_ref, do_ref, lse_ref,
    dq_ref, dk_ref, dv_ref, dk_acc, dv_acc,
):
    row_count = q_ref.shape[0]
    dk_acc[...] = jnp.zeros_like(dk_acc)
    dv_acc[...] = jnp.zeros_like(dv_acc)
    for block in range(row_count // ROW_BLOCK):
        first_row = block * ROW_BLOCK
        key_end = first_row + ROW_BLOCK
        allowed = block_mask(row_doc_ref, col_doc_ref, first_row, key_end)
        rows = pl.ds(first_row, ROW_BLOCK)

        def head_body(head, carry):
            cols = pl.ds(pl.multiple_of(head * HEAD_SIZE, HEAD_SIZE), HEAD_SIZE)
            query = q_ref[rows, cols]
            grad = do_ref[rows, cols]
            keys = k_ref[:key_end, :]
            values = v_ref[:key_end, :]
            log_total = lse_ref[0, head, rows, :][:, :1]
            scores = lax.dot_general(query, keys, NT_DIMS, preferred_element_type=jnp.float32) * factor
            scores = jnp.where(allowed, scores, MASKED)
            weights = jnp.exp(scores - log_total)
            dv_acc[:key_end, :] += jnp.dot(
                weights.astype(jnp.bfloat16).T, grad, preferred_element_type=jnp.float32
            )
            weight_grad = lax.dot_general(grad, values, NT_DIMS, preferred_element_type=jnp.float32)
            diagonal = jnp.sum(
                grad.astype(jnp.float32) * o_ref[rows, cols].astype(jnp.float32), axis=1, keepdims=True
            )
            score_grad = (weights * (weight_grad - diagonal) * factor).astype(jnp.bfloat16)
            dq_ref[rows, cols] = jnp.dot(score_grad, keys, preferred_element_type=jnp.float32).astype(
                dq_ref.dtype
            )
            dk_acc[:key_end, :] += jnp.dot(score_grad.T, query, preferred_element_type=jnp.float32)
            return carry

        lax.fori_loop(0, GROUP, head_body, 0)
    dk_ref[...] = dk_acc[...].astype(dk_ref.dtype)
    dv_ref[...] = dv_acc[...].astype(dv_ref.dtype)


def doc_views(doc_ids):
    return doc_ids[:, None], doc_ids[None, :]


def attention_forward(query, keys, values, doc_ids, factor):
    row_count = query.shape[0]
    groups = keys.shape[1] // HEAD_SIZE
    width = GROUP * HEAD_SIZE
    row_doc, col_doc = doc_views(doc_ids)
    flops = 4 * groups * GROUP * row_count * row_count * HEAD_SIZE
    return pl.pallas_call(
        functools.partial(forward_kernel, factor),
        grid=(groups,),
        in_specs=[
            pl.BlockSpec((row_count, width), lambda g: (0, g)),
            pl.BlockSpec((row_count, HEAD_SIZE), lambda g: (0, g)),
            pl.BlockSpec((row_count, HEAD_SIZE), lambda g: (0, g)),
            pl.BlockSpec((row_count, 1), lambda g: (0, 0)),
            pl.BlockSpec((1, row_count), lambda g: (0, 0)),
        ],
        out_specs=[
            pl.BlockSpec((row_count, width), lambda g: (0, g)),
            pl.BlockSpec((1, GROUP, row_count, HEAD_SIZE), lambda g: (g, 0, 0, 0)),
        ],
        out_shape=[
            jax.ShapeDtypeStruct(query.shape, query.dtype),
            jax.ShapeDtypeStruct((groups, GROUP, row_count, HEAD_SIZE), jnp.float32),
        ],
        compiler_params=pltpu.CompilerParams(vmem_limit_bytes=48 * 1024 * 1024),
        cost_estimate=pl.CostEstimate(
            flops=flops // 2, transcendentals=groups * GROUP * row_count * row_count // 2,
            bytes_accessed=4 * query.size + 8 * keys.size + 8 * groups * GROUP * row_count * HEAD_SIZE,
        ),
    )(query, keys, values, row_doc, col_doc)


def attention_backward_group(group, query, keys, values, doc_ids, attn, grad, lse, factor):
    row_count = query.shape[0]
    width = GROUP * HEAD_SIZE
    row_doc, col_doc = doc_views(doc_ids)
    flops = 10 * GROUP * row_count * row_count * HEAD_SIZE
    return pl.pallas_call(
        functools.partial(backward_kernel, factor),
        grid=(1,),
        in_specs=[
            pl.BlockSpec((row_count, width), lambda g: (0, group)),
            pl.BlockSpec((row_count, HEAD_SIZE), lambda g: (0, group)),
            pl.BlockSpec((row_count, HEAD_SIZE), lambda g: (0, group)),
            pl.BlockSpec((row_count, 1), lambda g: (0, 0)),
            pl.BlockSpec((1, row_count), lambda g: (0, 0)),
            pl.BlockSpec((row_count, width), lambda g: (0, group)),
            pl.BlockSpec((row_count, width), lambda g: (0, group)),
            pl.BlockSpec((1, GROUP, row_count, HEAD_SIZE), lambda g: (group, 0, 0, 0)),
        ],
        out_specs=[
            pl.BlockSpec((row_count, width), lambda g: (0, 0)),
            pl.BlockSpec((row_count, HEAD_SIZE), lambda g: (0, 0)),
            pl.BlockSpec((row_count, HEAD_SIZE), lambda g: (0, 0)),
        ],
        out_shape=[
            jax.ShapeDtypeStruct((row_count, width), query.dtype),
            jax.ShapeDtypeStruct((row_count, HEAD_SIZE), keys.dtype),
            jax.ShapeDtypeStruct((row_count, HEAD_SIZE), keys.dtype),
        ],
        scratch_shapes=[
            pltpu.VMEM((row_count, HEAD_SIZE), jnp.float32),
            pltpu.VMEM((row_count, HEAD_SIZE), jnp.float32),
        ],
        compiler_params=pltpu.CompilerParams(vmem_limit_bytes=48 * 1024 * 1024),
        cost_estimate=pl.CostEstimate(
            flops=flops // 2, transcendentals=GROUP * row_count * row_count // 2,
            bytes_accessed=2 * 4 * row_count * width + 4 * row_count * HEAD_SIZE * 4
            + 4 * GROUP * row_count * HEAD_SIZE,
        ),
    )(query, keys, values, row_doc, col_doc, attn, grad, lse)


def attach_counts(out_weight, local_counts):
    high = (local_counts // COUNT_BASE).astype(out_weight.dtype)
    low = (local_counts % COUNT_BASE).astype(out_weight.dtype)
    rows = jnp.zeros((16, out_weight.shape[1]), out_weight.dtype)
    rows = rows.at[0, :LANGS].set(high).at[1, :LANGS].set(low)
    return jnp.concatenate([out_weight, rows], axis=0)


def gather_features(block):
    tensor_size = lax.axis_size("tensor")
    me = lax.axis_index("tensor")
    arrived = [(me, block)]
    for shift in range(1, tensor_size):
        pairs = [(index, (index + shift) % tensor_size) for index in range(tensor_size)]
        moved = lax.ppermute(block, "tensor", pairs)
        arrived.append(((me - shift) % tensor_size, moved))
    return arrived


def place_blocks(blocks, rows, width):
    full = jnp.zeros((rows, len(blocks) * width), blocks[0][1].dtype)
    for source, part in blocks:
        full = lax.dynamic_update_slice(full, part, (0, source * width))
    return full


def layer(query, keys, values, out_weight, loss_grad, lengths, languages, labels):
    factor = 1.0 / math.sqrt(HEAD_SIZE)
    row_count = query.shape[0]
    doc_ids = token_docs(lengths[0], row_count).astype(jnp.int32)
    attention_result, log_rows = attention_forward(query, keys, values, doc_ids, factor)
    token_lang = jnp.sum(
        jnp.where(
            doc_ids[:, None] == jnp.arange(DOCS, dtype=jnp.int32)[None, :], languages[0][None, :], 0
        ),
        axis=1,
    )
    counted = labels != -100
    lang_match = token_lang[:, None] == jnp.arange(LANGS, dtype=jnp.int32)[None, :]
    local_counts = jnp.sum((lang_match & counted[:, None]).astype(jnp.int32), axis=0)
    head_rows = out_weight.shape[0] // 2
    gathered = lax.all_gather(
        attach_counts(out_weight[:head_rows], local_counts), "dp", axis=1, tiled=True
    )
    rest = lax.all_gather(out_weight[head_rows:], "dp", axis=1, tiled=True)
    full_weight = jnp.concatenate([gathered[:head_rows], rest], axis=0)
    code = gathered[head_rows : head_rows + 2].astype(jnp.float32)
    code = code.reshape(2, lax.axis_size("dp"), out_weight.shape[1])[:, :, :LANGS]
    counts = jnp.sum(code[0] * COUNT_BASE + code[1], axis=0)
    lang_weight = jnp.sqrt(jnp.sum(counts) / (LANGS * jnp.maximum(counts, 1.0)))
    token_weight = jnp.where(
        counted, jnp.sum(jnp.where(lang_match, lang_weight[None, :], 0.0), axis=1), 0.0
    )
    width = loss_grad.shape[1]
    weighted_blocks = [
        (source, (token_weight[:, None] * part.astype(jnp.float32)).astype(jnp.bfloat16))
        for source, part in gather_features(loss_grad)
    ]
    term_blocks = [
        (
            source,
            lax.dot_general(
                attention_result, part, (((0,), (0,)), ((), ())), preferred_element_type=jnp.float32
            ).astype(jnp.bfloat16),
        )
        for source, part in weighted_blocks
    ]
    local_term = place_blocks(term_blocks, attention_result.shape[1], width)
    projection_part = lax.psum_scatter(local_term, "dp", scatter_dimension=0, tiled=True)
    projection_gradient = lax.all_gather(projection_part, "dp", axis=0, tiled=True)
    weighted = place_blocks(weighted_blocks, loss_grad.shape[0], width)
    local_term, weighted = lax.optimization_barrier((local_term, weighted))
    out_grad = lax.dot_general(
        weighted,
        full_weight,
        (((1,), (1,)), ((), ())),
        preferred_element_type=jnp.float32,
    ).astype(jnp.bfloat16)

    parts = []
    for group in range(keys.shape[1] // HEAD_SIZE):
        parts.append(
            attention_backward_group(
                group, query, keys, values, doc_ids, attention_result, out_grad, log_rows, factor
            )
        )
    query_gradient, key_gradient, value_gradient = (
        jnp.concatenate([part[k] for part in parts], axis=1) for k in range(3)
    )
    return (attention_result, query_gradient, key_gradient, value_gradient, projection_gradient)


def solution(mesh):
    in_specs = (
        P("dp", "tensor"),
        P("dp", "tensor"),
        P("dp", "tensor"),
        P("tensor", "dp"),
        P("dp", "tensor"),
        P("dp", None),
        P("dp", None),
        P("dp"),
    )
    out_specs = (
        P("dp", "tensor"),
        P("dp", "tensor"),
        P("dp", "tensor"),
        P("dp", "tensor"),
        P("tensor", None),
    )
    return jax.shard_map(layer, mesh=mesh, in_specs=in_specs, out_specs=out_specs, check_vma=False)
```

profile of v0, /device:TPU:0, one launch (start us, length us, event | category | flops | bytes accessed | tf_op | source)
XLA Modules:
  0.0 290.9 jit_solution(17192412400375811156)
XLA Ops:
  10.1 1.6 fusion.21
  12.4 2.1 collective-permute-start
  14.5 3.6 %collective-permute-start.1 = (bf16[1024,640]{1,0:T(8,128)(2,1)}, bf16[1024,640]{1,0:T(8,128)(2,1)}, u32[]{:S(2)}, u32[]{:S(2)}) collective-permute-start(bf16[1024,640]{1,0:T(8,128)(2,1)} %param.16), channel_id=1, source_target_pairs={{0,2},{1,3},{2,0},{3,1},{4,6},{5,7},{6,4},{7,5},{8,10},{9,11},{10,... | collective-permute-start | bytes 3932168 | tf_op jit(solution)/shard_map/ppermute | solution.py:200
  19.3 1.7 copy-done
  23.2 30.7 %shard_map.119 = (bf16[1024,1280]{1,0:T(8,128)(2,1)}, f32[2,5,1024,128]{3,2,1,0:T(8,128)}) custom-call(bf16[1024,1280]{1,0:T(8,128)(2,1)S(1)} %copy-done, bf16[1024,256]{1,0:T(8,128)(2,1)S(1)} %copy-done.2, bf16[1024,256]{1,0:T(8,128)(2,1)S(1)} %copy-done.4, s32[1024,1]{1,0:T(8,128)S(1)} %copy.21.row_doc_ref, s32[1,1024]{1,0:T(1,128)S(1)} %bitcast.29), custom_call_target="tpu_custom_call" | custom-call | flops 2684354560 | bytes 17825792 | tf_op jit(solution)/shard_map/pallas_call | solution.py:119
  53.9 6.7 %all-gather.4.cloned.1.call-done = bf16[656,2560]{0,1:T(8,128)(2,1)} async-done(((bf16[656,80]{0,1:T(8,128)(2,1)}), bf16[656,2560]{0,1:T(8,128)(2,1)}) %all-gather.4.cloned.1.call-update) | async-done | bytes 3358736 | tf_op jit(solution)/shard_map/all_gather | solution.py:227
  60.6 1.1 slice.62
  63.5 3.5 %broadcast_in_dim.61 = bf16[1280,2560]{1,0:T(8,128)(2,1)} broadcast(bf16[]{:T(256)} %constant.116.clone.1), dimensions={} | broadcast | bytes 6553602 | tf_op jit(solution)/shard_map/broadcast_in_dim | solution.py:206
  67.3 3.6 %fusion.10 = bf16[1280,2560]{1,0:T(8,128)(2,1)} fusion(bf16[1280,2560]{1,0:T(8,128)(2,1)} %broadcast_in_dim.61, s32[]{:T(128)S(6)} %select_n.69, bf16[1024,1280]{1,0:T(8,128)(2,1)S(1)} %copy-done.6, bf16[1024,640]{1,0:T(8,128)(2,1)S(1)} %copy-done.9, f32[1024]{0:T(1024)S(1)} %broadcast_select_fusion), kind=kOutput, calls=%fused_computation.12 | convolution fusion | flops 1680506880 | bytes 5574660 | tf_op jit(solution)/shard_map/dot_general | solution.py:247
  71.0 3.6 %fusion.9 = bf16[1280,2560]{1,0:T(8,128)(2,1)} fusion(bf16[1280,2560]{1,0:T(8,128)(2,1)} %fusion.10, s32[]{:T(128)S(6)} %select_n.71, bf16[1024,1280]{1,0:T(8,128)(2,1)S(1)} %copy-done.6, bf16[1024,640]{1,0:T(8,128)(2,1)S(1)} %collective-permute-done, f32[1024]{0:T(1024)S(1)} %broadcast_select_fusion), kind=kOutput, calls=%fused_computation.10 | convolution fusion | flops 1680506880 | bytes 5574660 | tf_op jit(solution)/shard_map/dot_general | solution.py:247
  75.0 4.9 %fusion.8 = bf16[1280,2560]{1,0:T(8,128)(2,1)} fusion(bf16[1280,2560]{1,0:T(8,128)(2,1)} %fusion.9, s32[]{:T(128)S(6)} %select_n.73, bf16[1024,1280]{1,0:T(8,128)(2,1)S(1)} %copy-done.6, bf16[1024,640]{1,0:T(8,128)(2,1)} %collective-permute-done.1, f32[1024]{0:T(1024)S(1)} %broadcast_select_fusion), kind=kOutput, calls=%fused_computation.8 | convolution fusion | flops 1680506880 | bytes 5574660 | tf_op jit(solution)/shard_map/dot_general | solution.py:247
  79.9 4.9 %fusion.7 = bf16[1280,2560]{1,0:T(8,128)(2,1)} fusion(bf16[1280,2560]{1,0:T(8,128)(2,1)} %fusion.8, s32[]{:T(128)S(6)} %select_n.75, bf16[1024,1280]{1,0:T(8,128)(2,1)S(1)} %copy-done.6, bf16[1024,640]{1,0:T(8,128)(2,1)} %collective-permute-done.2, f32[1024]{0:T(1024)S(1)} %broadcast_select_fusion), kind=kOutput, calls=%fused_computation.6 | convolution fusion | flops 1680506880 | bytes 5574660 | tf_op jit(solution)/shard_map/dot_general | solution.py:247
  85.8 87.9 %reduce-scatter.2.cloned.1.call-done = bf16[40,2560]{1,0:T(8,128)(2,1)} async-done(((bf16[1280,2560]{1,0:T(8,128)(2,1)}), bf16[40,2560]{1,0:T(8,128)(2,1)}) %reduce-scatter.2.cloned.1.call-update) | async-done | bytes 204816 | tf_op jit(solution)/shard_map/reduce_scatter | solution.py:254
  174.8 1.8 fusion.13
  176.7 1.7 fusion.14
  178.4 2.3 copy-done.7
  180.7 2.0 slice.65
  182.8 38.0 %all-gather.6.cloned.1.call-done = bf16[640,2560]{0,1:T(8,128)(2,1)} async-done(((bf16[640,80]{0,1:T(8,128)(2,1)}), bf16[640,2560]{0,1:T(8,128)(2,1)}) %all-gather.6.cloned.1.call-update) | async-done | bytes 3276816 | tf_op jit(solution)/shard_map/all_gather | solution.py:230
  220.8 11.9 %fusion.4.do_ref = bf16[1024,1280]{1,0:T(8,128)(2,1)} fusion(bf16[1024,2560]{1,0:T(8,128)(2,1)} %copy-done.7, bf16[640,2560]{0,1:T(8,128)(2,1)} %all-gather.6.cloned.1.call-done, bf16[640,2560]{0,1:T(8,128)(2,1)} %slice.65), kind=kOutput, calls=%fused_computation.4 | convolution fusion | flops 6725304320 | bytes 14417920 | tf_op jit(solution)/shard_map/dot_general | solution.py:258
  232.7 21.4 %shard_map.121 = (bf16[1024,640]{1,0:T(8,128)(2,1)S(1)}, bf16[1024,128]{1,0:T(8,128)(2,1)S(1)}, bf16[1024,128]{1,0:T(8,128)(2,1)S(1)}) custom-call(bf16[1024,1280]{1,0:T(8,128)(2,1)S(1)} %copy-done.1, bf16[1024,256]{1,0:T(8,128)(2,1)S(1)} %copy-done.3, bf16[1024,256]{1,0:T(8,128)(2,1)S(1)} %copy-done.5, s32[1024,1]{1,0:T(8,128)S(1)} %copy.21.row_doc_ref, ...), custom_call_target="tpu_custom_call" | custom-call | flops 3355443200 | bytes 9961472 | tf_op jit(solution)/shard_map/pallas_call | solution.py:150
  254.1 21.4 %shard_map.120 = (bf16[1024,640]{1,0:T(8,128)(2,1)S(1)}, bf16[1024,128]{1,0:T(8,128)(2,1)S(1)}, bf16[1024,128]{1,0:T(8,128)(2,1)S(1)}) custom-call(bf16[1024,1280]{1,0:T(8,128)(2,1)S(1)} %copy-done.1, bf16[1024,256]{1,0:T(8,128)(2,1)S(1)} %copy-done.3, bf16[1024,256]{1,0:T(8,128)(2,1)S(1)} %copy-done.5, s32[1024,1]{1,0:T(8,128)S(1)} %copy.21.row_doc_ref, ...), custom_call_target="tpu_custom_call" | custom-call | flops 3355443200 | bytes 9961472 | tf_op jit(solution)/shard_map/pallas_call | solution.py:150
  275.5 1.1 pad_maximum_fusion.1
  276.6 1.7 pad_maximum_fusion
  278.3 6.1 %copy.35 = bf16[1280,2560]{1,0:T(8,128)(2,1)} copy(bf16[1280,2560]{1,0:T(8,128)(2,1)} %all-gather.8.cloned.1.call-done) | data formatting | bytes 13107200
  (54 shorter events, 11.5 us)
Async XLA Ops:
  7.2 53.4 %all-gather.4.cloned.1.call-start = ((), (), s32[]{:S(2)}) async-start(), calls=%async_computation.1 | async-start | bytes 4055040 | tf_op jit(solution)/shard_map/all_gather | solution.py:227
  12.4 161.3 %reduce-scatter.2.cloned.1.call-start = ((), (), s32[]{:S(2)}) async-start(), calls=%async_computation.3 | async-start | bytes 6758400 | tf_op jit(solution)/shard_map/reduce_scatter | solution.py:254
  12.4 58.6 %collective-permute-start = (bf16[1024,640]{1,0:T(8,128)(2,1)}, bf16[1024,640]{1,0:T(8,128)(2,1)S(1)}, u32[]{:S(2)}, u32[]{:S(2)}) collective-permute-start(bf16[1024,640]{1,0:T(8,128)(2,1)} %param.16), channel_id=1, source_target_pairs={{0,1},{1,2},{2,3},{3,0},{4,5},{5,6},{6,7},{7,4},{8,9},{9,10},{10,1... | collective-permute-start | bytes 3932168 | tf_op jit(solution)/shard_map/ppermute | solution.py:200
  14.5 60.5 %collective-permute-start.1 = (bf16[1024,640]{1,0:T(8,128)(2,1)}, bf16[1024,640]{1,0:T(8,128)(2,1)}, u32[]{:S(2)}, u32[]{:S(2)}) collective-permute-start(bf16[1024,640]{1,0:T(8,128)(2,1)} %param.16), channel_id=1, source_target_pairs={{0,2},{1,3},{2,0},{3,1},{4,6},{5,7},{6,4},{7,5},{8,10},{9,11},{10,... | collective-permute-start | bytes 3932168 | tf_op jit(solution)/shard_map/ppermute | solution.py:200
  18.1 61.8 %collective-permute-start.2 = (bf16[1024,640]{1,0:T(8,128)(2,1)}, bf16[1024,640]{1,0:T(8,128)(2,1)}, u32[]{:S(2)}, u32[]{:S(2)}) collective-permute-start(bf16[1024,640]{1,0:T(8,128)(2,1)} %param.16), channel_id=1, source_target_pairs={{0,3},{1,0},{2,1},{3,2},{4,7},{5,4},{6,5},{7,6},{8,11},{9,8},{10,9... | collective-permute-start | bytes 3932168 | tf_op jit(solution)/shard_map/ppermute | solution.py:200
  19.3 1.7 copy-start
  21.1 1.0 copy-start.2
  22.1 1.0 copy-start.4
  53.9 9.5 %copy-start.10 = (s32[1024]{0:T(1024)S(1)}, s32[1024]{0:T(1024)}, u32[]{:S(2)}) copy-start(s32[1024]{0:T(1024)} %param.19) | copy-start | bytes 12292
  63.4 3.5 %copy-start.6 = (bf16[1024,1280]{1,0:T(8,128)(2,1)S(1)}, bf16[1024,1280]{1,0:T(8,128)(2,1)}, u32[]{:S(2)}) copy-start(bf16[1024,1280]{1,0:T(8,128)(2,1)} %get-tuple-element.60.o_ref) | copy-start | bytes 7864324
  63.4 3.9 %copy-start.9 = (bf16[1024,640]{1,0:T(8,128)(2,1)S(1)}, bf16[1024,640]{1,0:T(8,128)(2,1)}, u32[]{:S(2)}) copy-start(bf16[1024,640]{1,0:T(8,128)(2,1)} %param.16) | copy-start | bytes 3932164
  84.8 136.0 %all-gather.6.cloned.1.call-start = ((), (), s32[]{:S(2)}) async-start(), calls=%async_computation.2 | async-start | bytes 3379200 | tf_op jit(solution)/shard_map/all_gather | solution.py:230
  85.5 192.7 %all-gather.8.cloned.1.call-start = ((), (), s32[]{:S(2)}) async-start(), calls=%async_computation.4 | async-start | bytes 6758400 | tf_op jit(solution)/shard_map/all_gather | solution.py:255
  174.8 5.9 %copy-start.8 = (bf16[656,2560]{0,1:T(8,128)(2,1)S(1)}, bf16[656,2560]{0,1:T(8,128)(2,1)}, u32[]{:S(2)}) copy-start(bf16[656,2560]{0,1:T(8,128)(2,1)} %all-gather.4.cloned.1.call-done) | copy-start | bytes 10076164
  178.4 2.4 copy-start.7
  182.8 49.9 %copy-start.1 = (bf16[1024,1280]{1,0:T(8,128)(2,1)S(1)}, bf16[1024,1280]{1,0:T(8,128)(2,1)}, u32[]{:S(2)}) copy-start(bf16[1024,1280]{1,0:T(8,128)(2,1)} %q_ref.5) | copy-start | bytes 7864324
  220.8 11.9 %copy-start.3 = (bf16[1024,256]{1,0:T(8,128)(2,1)S(1)}, bf16[1024,256]{1,0:T(8,128)(2,1)}, u32[]{:S(2)}) copy-start(bf16[1024,256]{1,0:T(8,128)(2,1)} %k_ref.5) | copy-start | bytes 1572868
  220.8 11.9 %copy-start.5 = (bf16[1024,256]{1,0:T(8,128)(2,1)S(1)}, bf16[1024,256]{1,0:T(8,128)(2,1)}, u32[]{:S(2)}) copy-start(bf16[1024,256]{1,0:T(8,128)(2,1)} %v_ref.5) | copy-start | bytes 1572868
Sparse Core Ops, SparseCore 0:
  12.5 48.0 all-gather.3
  84.9 88.7 reduce-scatter.1
  176.6 44.1 all-gather.5
  222.9 48.6 all-gather.7
where the time goes:
time: 292 us; the launch traced here: 291 us
  waiting for transfers between devices  134 us (46%)
  Pallas kernels  73.5 us (25%)
  matrix products  29 us (10%)
  local copies, waits for them, and re-layouts  22.5 us (8%)
  between operations  13.9 us (5%)
  other arithmetic  11.2 us (4%)
  starting transfers between devices  7.07 us (2%)
    reduce_scatter x1, waiting for transfers between devices, layer(): lax.psum_scatter(local_term, 'dp', scatter_dimension=0, tiled=True)  87.9 us
    pallas_call x2, Pallas kernels, attention_backward_group(): pl.pallas_call(functools.partial(backward_kernel, factor), grid=(1,), in_...  42.8 us
    all_gather x1, waiting for transfers between devices, layer(): rest = lax.all_gather(out_weight[head_rows:], 'dp', axis=1, tiled=True)  38 us
    pallas_call x1, Pallas kernels, attention_forward(): pl.pallas_call(functools.partial(forward_kernel, factor), grid=(groups,),...  30.7 us
    dot_general x4, matrix products, layer(): lax.dot_general(attention_result, part, (((0,), (0,)), ((), ())), preferr...  17 us
    unnamed x23, local copies, waits for them, and re-layouts  12.7 us
    dot_general x1, matrix products, layer(): lax.dot_general(weighted, full_weight, (((1,), (1,)), ((), ())), preferre...  11.9 us
    all_gather x1, waiting for transfers between devices, layer(): lax.all_gather(attach_counts(out_weight[:head_rows], local_counts), 'dp',...  6.73 us
  transfers between devices with their start and end apart: 7, of which 4 were waited for; matrix products, arithmetic and copies ran while one was open for 14% of the time, Pallas kernels for 25%

commit v1 on v0

--- a/solution.py
+++ b/solution.py
@@ -223,13 +223,12 @@
     counted = labels != -100
     lang_match = token_lang[:, None] == jnp.arange(LANGS, dtype=jnp.int32)[None, :]
     local_counts = jnp.sum((lang_match & counted[:, None]).astype(jnp.int32), axis=0)
-    head_rows = out_weight.shape[0] // 2
+    weight_rows = out_weight.shape[0]
     gathered = lax.all_gather(
-        attach_counts(out_weight[:head_rows], local_counts), "dp", axis=1, tiled=True
-    )
-    rest = lax.all_gather(out_weight[head_rows:], "dp", axis=1, tiled=True)
-    full_weight = jnp.concatenate([gathered[:head_rows], rest], axis=0)
-    code = gathered[head_rows : head_rows + 2].astype(jnp.float32)
+        attach_counts(out_weight, local_counts), "dp", axis=1, tiled=True
+    )
+    full_weight = gathered[:weight_rows]
+    code = gathered[weight_rows : weight_rows + 2].astype(jnp.float32)
     code = code.reshape(2, lax.axis_size("dp"), out_weight.shape[1])[:, :, :LANGS]
     counts = jnp.sum(code[0] * COUNT_BASE + code[1], axis=0)
     lang_weight = jnp.sqrt(jnp.sum(counts) / (LANGS * jnp.maximum(counts, 1.0)))

time: 292 us -> 250 us (0.86)
  waiting for transfers between devices: 134 us -> 97 us
  local copies, waits for them, and re-layouts: 22.5 us -> 17.5 us
    all_gather x2 -> x1, waiting for transfers between devices: 44.7 us -> 11.5 us  [layer(): lax.all_gather(attach_counts(out_weight, local_counts), 'dp', axis=1, til...]
    dot_general x1, matrix products: 11.9 us -> 8.17 us  [layer(): lax.dot_general(weighted, full_weight, (((1,), (1,)), ((), ())), preferre...]
    slice x3 -> x1, local copies, waits for them, and re-layouts: 4.78 us -> 1.13 us  [layer(): code = gathered[weight_rows:weight_rows + 2].astype(jnp.float32)]
    unnamed x23 -> x25, local copies, waits for them, and re-layouts: 12.7 us -> 11.3 us
  transfers between devices with their start and end apart: 7 -> 6, of which waited for: 4 -> 2; matrix products, arithmetic and copies ran while one was open for 14% -> 15% of each run, Pallas kernels for 25% -> 30%
where the time goes in v1:
time: 250 us; the launch traced here: 249 us
  waiting for transfers between devices  97 us (39%)
  Pallas kernels  73.8 us (30%)
  matrix products  26.5 us (11%)
  local copies, waits for them, and re-layouts  17.5 us (7%)
  between operations  13.9 us (6%)
  other arithmetic  13.5 us (5%)
  starting transfers between devices  7.03 us (3%)
    reduce_scatter x1, waiting for transfers between devices, layer(): lax.psum_scatter(local_term, 'dp', scatter_dimension=0, tiled=True)  85.5 us
    pallas_call x2, Pallas kernels, attention_backward_group(): pl.pallas_call(functools.partial(backward_kernel, factor), grid=(1,), in_...  43.1 us
    pallas_call x1, Pallas kernels, attention_forward(): pl.pallas_call(functools.partial(forward_kernel, factor), grid=(groups,),...  30.7 us
    dot_general x4, matrix products, layer(): lax.dot_general(attention_result, part, (((0,), (0,)), ((), ())), preferr...  18.3 us
    all_gather x1, waiting for transfers between devices, layer(): lax.all_gather(attach_counts(out_weight, local_counts), 'dp', axis=1, til...  11.5 us
    unnamed x25, local copies, waits for them, and re-layouts  11.3 us
    dot_general x1, matrix products, layer(): lax.dot_general(weighted, full_weight, (((1,), (1,)), ((), ())), preferre...  8.17 us
    ppermute x3, starting transfers between devices, gather_features(): moved = lax.ppermute(block, 'tensor', pairs)  6.69 us
  transfers between devices with their start and end apart: 6, of which 2 were waited for; matrix products, arithmetic and copies ran while one was open for 15% of the time, Pallas kernels for 30%

profile of v1, /device:TPU:0, one launch (start us, length us, event | category | flops | bytes accessed | tf_op | source)
XLA Modules:
  0.0 249.2 jit_solution(4652233529223921327)
XLA Ops:
  10.1 1.6 pad_maximum_fusion.3
  11.8 2.1 collective-permute-start
  13.9 3.6 %collective-permute-start.1 = (bf16[1024,640]{1,0:T(8,128)(2,1)}, bf16[1024,640]{1,0:T(8,128)(2,1)}, u32[]{:S(2)}, u32[]{:S(2)}) collective-permute-start(bf16[1024,640]{1,0:T(8,128)(2,1)} %param.16), channel_id=1, source_target_pairs={{0,2},{1,3},{2,0},{3,1},{4,6},{5,7},{6,4},{7,5},{8,10},{9,11},{10,... | collective-permute-start | bytes 3932168 | tf_op jit(solution)/shard_map/ppermute | solution.py:200
  18.7 1.7 copy-done
  20.4 1.0 copy-done.2
  21.5 1.0 copy-done.4
  22.5 30.7 %shard_map.119 = (bf16[1024,1280]{1,0:T(8,128)(2,1)}, f32[2,5,1024,128]{3,2,1,0:T(8,128)}) custom-call(bf16[1024,1280]{1,0:T(8,128)(2,1)S(1)} %copy-done, bf16[1024,256]{1,0:T(8,128)(2,1)S(1)} %copy-done.2, bf16[1024,256]{1,0:T(8,128)(2,1)S(1)} %copy-done.4, s32[1024,1]{1,0:T(8,128)S(1)} %copy.21.row_doc_ref, s32[1,1024]{1,0:T(1,128)S(1)} %bitcast.29), custom_call_target="tpu_custom_call" | custom-call | flops 2684354560 | bytes 17825792 | tf_op jit(solution)/shard_map/pallas_call | solution.py:119
  53.3 11.5 %all-gather.3.cloned.1.call-done = bf16[1296,2560]{0,1:T(8,128)(2,1)} async-done(((bf16[1296,80]{0,1:T(8,128)(2,1)}), bf16[1296,2560]{0,1:T(8,128)(2,1)}) %all-gather.3.cloned.1.call-update) | async-done | bytes 6635536 | tf_op jit(solution)/shard_map/all_gather | solution.py:227
  64.8 1.1 slice.54
  67.6 3.5 %broadcast_in_dim.61 = bf16[1280,2560]{1,0:T(8,128)(2,1)} broadcast(bf16[]{:T(256)} %constant.116.clone.1), dimensions={} | broadcast | bytes 6553602 | tf_op jit(solution)/shard_map/broadcast_in_dim | solution.py:206
  71.5 3.6 %fusion.8 = bf16[1280,2560]{1,0:T(8,128)(2,1)} fusion(bf16[1280,2560]{1,0:T(8,128)(2,1)} %broadcast_in_dim.61, s32[]{:T(128)S(6)} %select_n.69, bf16[1024,1280]{1,0:T(8,128)(2,1)S(1)} %copy-done.6, bf16[1024,640]{1,0:T(8,128)(2,1)S(1)} %copy-done.7, f32[1024]{0:T(1024)S(1)} %broadcast_select_fusion), kind=kOutput, calls=%fused_computation.10 | convolution fusion | flops 1680506880 | bytes 5574660 | tf_op jit(solution)/shard_map/dot_general | solution.py:246
  75.1 4.9 %fusion.7 = bf16[1280,2560]{1,0:T(8,128)(2,1)} fusion(bf16[1280,2560]{1,0:T(8,128)(2,1)} %fusion.8, s32[]{:T(128)S(6)} %select_n.71, bf16[1024,1280]{1,0:T(8,128)(2,1)S(1)} %copy-done.6, bf16[1024,640]{1,0:T(8,128)(2,1)} %collective-permute-done, f32[1024]{0:T(1024)S(1)} %broadcast_select_fusion), kind=kOutput, calls=%fused_computation.8 | convolution fusion | flops 1680506880 | bytes 5574660 | tf_op jit(solution)/shard_map/dot_general | solution.py:246
  80.0 4.9 %fusion.6 = bf16[1280,2560]{1,0:T(8,128)(2,1)} fusion(bf16[1280,2560]{1,0:T(8,128)(2,1)} %fusion.7, s32[]{:T(128)S(6)} %select_n.73, bf16[1024,1280]{1,0:T(8,128)(2,1)S(1)} %copy-done.6, bf16[1024,640]{1,0:T(8,128)(2,1)} %collective-permute-done.1, f32[1024]{0:T(1024)S(1)} %broadcast_select_fusion), kind=kOutput, calls=%fused_computation.6 | convolution fusion | flops 1680506880 | bytes 5574660 | tf_op jit(solution)/shard_map/dot_general | solution.py:246
  84.9 4.9 %fusion.5 = bf16[1280,2560]{1,0:T(8,128)(2,1)} fusion(bf16[1280,2560]{1,0:T(8,128)(2,1)} %fusion.6, s32[]{:T(128)S(6)} %select_n.75, bf16[1024,1280]{1,0:T(8,128)(2,1)S(1)} %copy-done.6, bf16[1024,640]{1,0:T(8,128)(2,1)} %collective-permute-done.2, f32[1024]{0:T(1024)S(1)} %broadcast_select_fusion), kind=kOutput, calls=%fused_computation.4 | convolution fusion | flops 1680506880 | bytes 5574660 | tf_op jit(solution)/shard_map/dot_general | solution.py:246
  90.1 85.5 %reduce-scatter.2.cloned.1.call-done = bf16[40,2560]{1,0:T(8,128)(2,1)} async-done(((bf16[1280,2560]{1,0:T(8,128)(2,1)}), bf16[40,2560]{1,0:T(8,128)(2,1)}) %reduce-scatter.2.cloned.1.call-update) | async-done | bytes 204816 | tf_op jit(solution)/shard_map/reduce_scatter | solution.py:253
  177.3 1.8 fusion.10
  179.1 1.7 fusion.11
  180.8 1.7 fusion.12
  182.6 8.2 %fusion.2.do_ref = bf16[1024,1280]{1,0:T(8,128)(2,1)} fusion(bf16[1024,2560]{1,0:T(8,128)(2,1)S(1)} %fusion.12, bf16[1296,2560]{0,1:T(8,128)(2,1)S(1)} %bitcast.34), kind=kOutput, calls=%fused_computation.2 | convolution fusion | flops 6712197120 | bytes 14417920 | tf_op jit(solution)/shard_map/dot_general | solution.py:257
  190.8 21.4 %shard_map.121 = (bf16[1024,640]{1,0:T(8,128)(2,1)S(1)}, bf16[1024,128]{1,0:T(8,128)(2,1)S(1)}, bf16[1024,128]{1,0:T(8,128)(2,1)S(1)}) custom-call(bf16[1024,1280]{1,0:T(8,128)(2,1)S(1)} %copy-done.1, bf16[1024,256]{1,0:T(8,128)(2,1)S(1)} %copy-done.3, bf16[1024,256]{1,0:T(8,128)(2,1)S(1)} %copy-done.5, s32[1024,1]{1,0:T(8,128)S(1)} %copy.21.row_doc_ref, ...), custom_call_target="tpu_custom_call" | custom-call | flops 3355443200 | bytes 9961472 | tf_op jit(solution)/shard_map/pallas_call | solution.py:150
  212.2 21.6 %shard_map.120 = (bf16[1024,640]{1,0:T(8,128)(2,1)S(1)}, bf16[1024,128]{1,0:T(8,128)(2,1)S(1)}, bf16[1024,128]{1,0:T(8,128)(2,1)S(1)}) custom-call(bf16[1024,1280]{1,0:T(8,128)(2,1)S(1)} %copy-done.1, bf16[1024,256]{1,0:T(8,128)(2,1)S(1)} %copy-done.3, bf16[1024,256]{1,0:T(8,128)(2,1)S(1)} %copy-done.5, s32[1024,1]{1,0:T(8,128)S(1)} %copy.21.row_doc_ref, ...), custom_call_target="tpu_custom_call" | custom-call | flops 3355443200 | bytes 9961472 | tf_op jit(solution)/shard_map/pallas_call | solution.py:150
  233.8 1.1 pad_maximum_fusion.1
  234.9 1.7 pad_maximum_fusion
  236.6 6.1 %copy.35 = bf16[1280,2560]{1,0:T(8,128)(2,1)} copy(bf16[1280,2560]{1,0:T(8,128)(2,1)} %all-gather.5.cloned.1.call-done) | data formatting | bytes 13107200
  (52 shorter events, 8.2 us)
Async XLA Ops:
  7.2 57.6 %all-gather.3.cloned.1.call-start = ((), (), s32[]{:S(2)}) async-start(), calls=%async_computation.1 | async-start | bytes 7434240 | tf_op jit(solution)/shard_map/all_gather | solution.py:227
  11.7 163.8 %reduce-scatter.2.cloned.1.call-start = ((), (), s32[]{:S(2)}) async-start(), calls=%async_computation.2 | async-start | bytes 6758400 | tf_op jit(solution)/shard_map/reduce_scatter | solution.py:253
  11.8 63.3 %collective-permute-start = (bf16[1024,640]{1,0:T(8,128)(2,1)}, bf16[1024,640]{1,0:T(8,128)(2,1)}, u32[]{:S(2)}, u32[]{:S(2)}) collective-permute-start(bf16[1024,640]{1,0:T(8,128)(2,1)} %param.16), channel_id=1, source_target_pairs={{0,1},{1,2},{2,3},{3,0},{4,5},{5,6},{6,7},{7,4},{8,9},{9,10},{10,1... | collective-permute-start | bytes 3932168 | tf_op jit(solution)/shard_map/ppermute | solution.py:200
  13.9 66.1 %collective-permute-start.1 = (bf16[1024,640]{1,0:T(8,128)(2,1)}, bf16[1024,640]{1,0:T(8,128)(2,1)}, u32[]{:S(2)}, u32[]{:S(2)}) collective-permute-start(bf16[1024,640]{1,0:T(8,128)(2,1)} %param.16), channel_id=1, source_target_pairs={{0,2},{1,3},{2,0},{3,1},{4,6},{5,7},{6,4},{7,5},{8,10},{9,11},{10,... | collective-permute-start | bytes 3932168 | tf_op jit(solution)/shard_map/ppermute | solution.py:200
  17.5 67.4 %collective-permute-start.2 = (bf16[1024,640]{1,0:T(8,128)(2,1)}, bf16[1024,640]{1,0:T(8,128)(2,1)}, u32[]{:S(2)}, u32[]{:S(2)}) collective-permute-start(bf16[1024,640]{1,0:T(8,128)(2,1)} %param.16), channel_id=1, source_target_pairs={{0,3},{1,0},{2,1},{3,2},{4,7},{5,4},{6,5},{7,6},{8,11},{9,8},{10,9... | collective-permute-start | bytes 3932168 | tf_op jit(solution)/shard_map/ppermute | solution.py:200
  18.7 1.7 copy-start
  20.4 1.0 copy-start.2
  21.5 1.0 copy-start.4
  53.3 14.3 %copy-start.9 = (s32[1024]{0:T(1024)S(1)}, s32[1024]{0:T(1024)}, u32[]{:S(2)}) copy-start(s32[1024]{0:T(1024)} %param.19) | copy-start | bytes 12292
  67.6 3.5 %copy-start.6 = (bf16[1024,1280]{1,0:T(8,128)(2,1)S(1)}, bf16[1024,1280]{1,0:T(8,128)(2,1)}, u32[]{:S(2)}) copy-start(bf16[1024,1280]{1,0:T(8,128)(2,1)} %get-tuple-element.58.o_ref) | copy-start | bytes 7864324
  67.6 3.9 %copy-start.7 = (bf16[1024,640]{1,0:T(8,128)(2,1)S(1)}, bf16[1024,640]{1,0:T(8,128)(2,1)}, u32[]{:S(2)}) copy-start(bf16[1024,640]{1,0:T(8,128)(2,1)} %param.16) | copy-start | bytes 3932164
  89.8 146.8 %all-gather.5.cloned.1.call-start = ((), (), s32[]{:S(2)}) async-start(), calls=%async_computation.3 | async-start | bytes 6758400 | tf_op jit(solution)/shard_map/all_gather | solution.py:254
  175.6 1.3 copy-start.8
  175.6 6.9 %slice-start = ((s8[7208960]{0:T(1024)(128)(4,1)}), s8[4194304]{0:T(1024)(128)(4,1)S(1)}, s32[]{:S(2)}) async-start(s8[7208960]{0:T(1024)(128)(4,1)} %bitcast.33), calls=%async_computation.4 | async-start | bytes 8388608
  177.3 5.3 %slice-start.1 = ((s8[7208960]{0:T(1024)(128)(4,1)}), s8[3014656]{0:T(1024)(128)(4,1)S(1)}, s32[]{:S(2)}) async-start(s8[7208960]{0:T(1024)(128)(4,1)} %bitcast.33), calls=%async_computation.5 | async-start | bytes 6029312
  182.5 8.2 %copy-start.1 = (bf16[1024,1280]{1,0:T(8,128)(2,1)S(1)}, bf16[1024,1280]{1,0:T(8,128)(2,1)}, u32[]{:S(2)}) copy-start(bf16[1024,1280]{1,0:T(8,128)(2,1)} %q_ref.5) | copy-start | bytes 7864324
  182.6 8.2 %copy-start.3 = (bf16[1024,256]{1,0:T(8,128)(2,1)S(1)}, bf16[1024,256]{1,0:T(8,128)(2,1)}, u32[]{:S(2)}) copy-start(bf16[1024,256]{1,0:T(8,128)(2,1)} %k_ref.5) | copy-start | bytes 1572868
  182.6 8.2 %copy-start.5 = (bf16[1024,256]{1,0:T(8,128)(2,1)S(1)}, bf16[1024,256]{1,0:T(8,128)(2,1)}, u32[]{:S(2)}) copy-start(bf16[1024,256]{1,0:T(8,128)(2,1)} %v_ref.5) | copy-start | bytes 1572868
Sparse Core Ops, SparseCore 0:
  11.8 52.8 all-gather.2
  89.9 85.5 reduce-scatter.1
  177.8 48.6 all-gather.4
